TPU v7x, 512 devices: a whole 4x4x16 slice. The times are simulated.
512 devices in a mesh: req: 128 (over z, y, core), wt: 4 (over x).
Axes of the slice: x: 4, y: 4, z: 16, core: 2. Of those that a mesh axis runs over, the one named last changes fastest.
Arguments:
- hidden_in: bfloat16 [32768, 5120], P('req', 'wt'), may hold values from -6 to 6
- queries: bfloat16 [32768, 5120], P('req', 'wt'), as said below
- key_proj: bfloat16 [32768, 5120], P('req', 'wt'), as said below
- values: bfloat16 [32768, 5120], P('req', 'wt'), may hold values from -6 to 6
- query_gain: float32 [5120], P('wt'), may hold values from 0.1 to 1.9
- key_gain: float32 [5120], P('wt'), may hold values from 0.1 to 1.9
- attn_gain: float32 [5120], P('wt'), may hold values from 0.1 to 1.9
- gate_w: bfloat16 [5120, 13824], P('wt', 'req'), may hold values from -0.078125 to 0.078125
- up_w: bfloat16 [5120, 13824], P('wt', 'req'), may hold values from -0.078125 to 0.078125
- lengths: int32 [128], replicated, may hold values from 1 to 256, 4608 in all
- assign: int32 [128], replicated, may hold values from 0 to 127, each once
- page_table: int32 [128, 2], P('req'), may hold values from 0 to 1, each once within a row
Outputs:
- gated: bfloat16 [128, 36, 13824], P(None, 'wt', 'req')
- key_cache: bfloat16 [256, 128, 5120], P('req', None, 'wt')
- value_cache: bfloat16 [256, 128, 5120], P('req', None, 'wt')
Inputs may be any that keep to these rules, and one draw needn't show every extreme that they name: lengths sum to 4608 and at least one request has exactly 256 tokens. `assign`: each device of req serves exactly one request. `page_table`: each row names each of the 2 pages of one device once. `queries`: real-valued entries within -24 to 24. `key_proj`: real-valued entries within -24 to 24.
All inputs are finite; a program needn't handle non-finite values.
Results may differ from a plain program's by a relative error of at most 0.013.
Values may be sent and summed in bfloat16 or wider, within the bound.
No kernel may reach another device: no remote copies, remote signals or barrier semaphores. Data moves between devices by JAX's collectives and lax.ppermute only.
A program may use at most 128 MiB of HBM per device.

v0:
```python
import jax
import jax.numpy as jnp
from jax import lax
from jax.sharding import PartitionSpec as P

D = 5120
HD = 128
PAGE = 128
LIVE = 36
EPS = 1e-06
THETA = 500000.0


def rope_tables(row_count, head_width):
    half_width = head_width // 2
    frequency = THETA ** (-(jnp.arange(half_width, dtype=jnp.float32) * 2.0 / head_width))
    angles = jnp.arange(row_count, dtype=jnp.float32)[:, None] * frequency[None, :]
    return (jnp.cos(angles), jnp.sin(angles))


def rotate(heads_in, cosine, sine_table):
    half_width = heads_in.shape[-1] // 2
    leading = heads_in[..., :half_width]
    trailing = heads_in[..., half_width:]
    cos_b = cosine[:, None, :]
    sin_b = sine_table[:, None, :]
    return jnp.concatenate(
        [leading * cos_b - trailing * sin_b, trailing * cos_b + leading * sin_b], axis=-1
    )


def deal_rows(source, owner_start, owner_len, device, owners, live_rows):
    slot_count = source.shape[0]
    feature_count = source.shape[1]
    per_peer = slot_count // owners
    column = jnp.arange(per_peer, dtype=jnp.int32)[None, :]
    target_dev = jnp.arange(owners, dtype=jnp.int32)[:, None]
    my_start = owner_start[device]
    my_length = owner_len[device]
    local_index = (target_dev - my_start) % owners + owners * column
    usable = local_index < my_length
    picked = jnp.where(
        usable[:, :, None],
        source[jnp.minimum(local_index, slot_count - 1)],
        jnp.zeros((), source.dtype),
    )
    arrived = lax.all_to_all(picked, "req", split_axis=0, concat_axis=0, tiled=True)
    src_start = owner_start[:, None]
    src_length = owner_len[:, None]
    sent_index = (device - src_start) % owners + owners * column
    landing = jnp.where(
        sent_index < src_length, (src_start + sent_index - device) // owners, live_rows
    )
    packed = jnp.zeros((live_rows, feature_count), source.dtype)
    return packed.at[landing.reshape(-1)].set(arrived.reshape(-1, feature_count), mode="drop")


def per_device(
    hidden_in,
    queries,
    key_proj,
    values,
    query_gain,
    key_gain,
    attn_gain,
    gate_w,
    up_w,
    lengths,
    assign,
    page_table,
):
    slot_count = hidden_in.shape[0]
    feature_count = hidden_in.shape[1]
    owners = lax.axis_size("req")
    device = lax.axis_index("req")
    head_count = feature_count // HD
    unit_count = gate_w.shape[1]
    owner_req = jnp.zeros((owners,), jnp.int32).at[assign].set(jnp.arange(owners, dtype=jnp.int32))
    starts = jnp.cumsum(lengths) - lengths
    owner_start = starts[owner_req]
    owner_len = lengths[owner_req]
    my_length = owner_len[device]
    query_f = queries.astype(jnp.float32)
    key_f = key_proj.astype(jnp.float32)
    query_sq, key_sq = lax.psum(
        (jnp.sum(query_f * query_f, axis=1), jnp.sum(key_f * key_f, axis=1)), "wt"
    )
    query_n = query_f * lax.rsqrt(query_sq / D + EPS)[:, None] * query_gain
    key_n = key_f * lax.rsqrt(key_sq / D + EPS)[:, None] * key_gain
    cosine, sine_table = rope_tables(slot_count, HD)
    query_r = rotate(query_n.reshape(slot_count, head_count, HD), cosine, sine_table).astype(
        jnp.bfloat16
    )
    key_r = rotate(key_n.reshape(slot_count, head_count, HD), cosine, sine_table).astype(
        jnp.bfloat16
    )
    scores = jnp.einsum(
        "qhd,khd->hqk", query_r, key_r, preferred_element_type=jnp.float32
    ) * HD ** (-0.5)
    position = jnp.arange(slot_count, dtype=jnp.int32)
    allowed = (position[None, :] <= position[:, None]) & (position[None, :] < my_length)
    scores = jnp.where(allowed[None], scores, -jnp.inf)
    row_peak = jnp.max(scores, axis=2, keepdims=True)
    expd = jnp.exp(scores - row_peak)
    probabilities = (expd / jnp.sum(expd, axis=2, keepdims=True)).astype(jnp.bfloat16)
    value_heads = values.reshape(slot_count, head_count, HD)
    attended = jnp.einsum(
        "hqk,khd->qhd", probabilities, value_heads, preferred_element_type=jnp.float32
    )
    attended = attended.astype(jnp.bfloat16).reshape(slot_count, feature_count)
    attended_f = attended.astype(jnp.float32)
    attn_sq = lax.psum(jnp.sum(attended_f * attended_f, axis=1), "wt")
    layer_rows = (
        hidden_in.astype(jnp.float32)
        + attended_f * lax.rsqrt(attn_sq / D + EPS)[:, None] * attn_gain
    ).astype(jnp.bfloat16)
    live_mask = (position < my_length)[:, None]
    page_count = slot_count // PAGE
    zero_value = jnp.zeros((), jnp.bfloat16)
    key_pages = jnp.where(live_mask, key_r.reshape(slot_count, feature_count), zero_value).reshape(
        page_count, PAGE, feature_count
    )
    value_pages = jnp.where(live_mask, values, zero_value).reshape(page_count, PAGE, feature_count)
    placement = page_table[0]
    key_cache = jnp.zeros_like(key_pages).at[placement].set(key_pages)
    value_cache = jnp.zeros_like(value_pages).at[placement].set(value_pages)
    regrouped = deal_rows(layer_rows, owner_start, owner_len, device, owners, LIVE)
    piece = lax.all_gather(regrouped, "req", axis=0, tiled=True)
    stacked = jnp.stack(
        [
            jnp.dot(piece, gate_w, preferred_element_type=jnp.float32),
            jnp.dot(piece, up_w, preferred_element_type=jnp.float32),
        ]
    )
    stacked = stacked.reshape(2, owners, LIVE, unit_count)
    gate_part, up_part = (
        lax.psum_scatter(stacked[0], "wt", scatter_dimension=1, tiled=True),
        lax.psum_scatter(stacked[1], "wt", scatter_dimension=1, tiled=True),
    )
    gated = (jax.nn.silu(gate_part) * up_part).astype(jnp.bfloat16)
    return (gated, key_cache, value_cache)


def solution(mesh):
    placed = (
        P("req", "wt"),
        P("req", "wt"),
        P("req", "wt"),
        P("req", "wt"),
        P("wt"),
        P("wt"),
        P("wt"),
        P("wt", "req"),
        P("wt", "req"),
        P(),
        P(),
        P("req", None),
    )
    return jax.shard_map(
        per_device,
        mesh=mesh,
        in_specs=placed,
        out_specs=(P(None, "wt", "req"), P("req", None, "wt"), P("req", None, "wt")),
        check_vma=False,
    )
```

profile of v0, /device:TPU:1, one launch (start us, length us, event | category | flops | bytes accessed | tf_op | source)
XLA Modules:
  0.0 378.9 jit_solution(4246838663136592697)
XLA Ops:
  7.2 1.4 copy.56
  9.3 9.3 %all-reduce = (f32[256]{0:T(256)S(1)}, f32[256]{0:T(256)S(1)}) all-reduce(f32[256]{0:T(256)S(1)} %fusion.5, f32[256]{0:T(256)S(1)} %fusion.3), channel_id=1, replica_groups=mesh['req'=128,'wt'=4] {'wt'}, use_global_device_ids=true, to_apply=%region_5.6 | all-reduce | flops 512 | bytes 4096 | tf_op jit(solution)/shard_map/psum | solution.py:85
  19.8 1.5 copy.78
  21.3 1.5 copy.79
  24.5 1.5 copy.76
  26.0 2.6 copy.77
  29.7 1.2 gather_fusion.1
  33.2 1.9 multiply_subtract_fusion
  36.5 1.5 subtract_convert_fusion
  38.0 4.1 %fusion.38 = (f32[10,256]{1,0:T(8,128)S(1)}, f32[10,256,256]{1,2,0:T(8,128)}) fusion(pred[256,256]{0,1:T(8,128)(4,1)S(1)} %fusion.14, bf16[256,10,128]{2,0,1:T(8,128)(2,1)S(1)} %maximum_convert_fusion, bf16[256,10,64]{2,0,1:T(8,128)(2,1)} %get-tuple-element.9, bf16[256,10,64]{2,0,1:T(8,128)(2,1)} %get-tuple-element.8), kind=kOutput, calls=%fused_computation.86 | convolution fusion | flops 171704576 | bytes 4007936 | tf_op jit(solution)/shard_map/sub | solution.py:104
  42.0 3.2 multiply_reduce_fusion
  45.2 1.7 copy.64
  47.0 6.0 %psum.23 = f32[256]{0:T(256)S(1)} all-reduce(f32[256]{0:T(256)S(1)} %get-tuple-element.22), channel_id=1, replica_groups=mesh['req'=128,'wt'=4] {'wt'}, use_global_device_ids=true, to_apply=%region_9.10 | all-reduce | flops 256 | bytes 2048 | tf_op jit(solution)/shard_map/psum | solution.py:112
  53.4 1.2 gather_fusion
  56.1 1.4 add_convert_fusion
  57.5 1.2 gather_fusion.2
  59.8 1.5 broadcast_select_fusion
  61.3 23.5 %all-to-all-start = ((bf16[128,2,1280]{2,1,0:T(2,128)(2,1)}), bf16[128,2,1280]{2,1,0:T(2,128)(2,1)S(1)}, u32[]{:S(2)}, u32[]{:S(2)}) async-start(bf16[128,2,1280]{2,1,0:T(2,128)(2,1)} %broadcast_select_fusion), calls=%async_computation | async-start | bytes 1310720 | tf_op jit(solution)/shard_map/all_to_all | solution.py:47
  85.5 35.7 %all-to-all-done = bf16[128,2,1280]{2,1,0:T(2,128)(2,1)S(1)} async-done(((bf16[128,2,1280]{2,1,0:T(2,128)(2,1)}), bf16[128,2,1280]{2,1,0:T(2,128)(2,1)S(1)}, u32[]{:S(2)}, u32[]{:S(2)}) %all-to-all-start) | async-done | bytes 655392 | tf_op jit(solution)/shard_map/all_to_all | solution.py:47
  121.5 2.2 scatter_custom_fusion.1
  123.8 146.6 %all-gather.3.cloned.1.call-done = bf16[128,36,1280]{2,1,0:T(8,128)(2,1)} async-done(((bf16[1,36,1280]{2,1,0:T(8,128)(2,1)}), bf16[128,36,1280]{2,1,0:T(8,128)(2,1)}) %all-gather.3.cloned.1.call-update) | async-done | bytes 11796496 | tf_op jit(solution)/shard_map/all_gather | solution.py:128
  270.4 16.9 %reshape.488 = bf16[4608,1280]{1,0:T(8,128)(2,1)} reshape(bf16[128,36,1280]{2,1,0:T(8,128)(2,1)} %all-gather.3.cloned.1.call-done) | data formatting | bytes 23592960
  287.3 6.1 %fusion.41 = f32[4608,108]{1,0:T(8,128)S(1)} fusion(bf16[4608,1280]{1,0:T(8,128)(2,1)} %reshape.488, bf16[1280,108]{0,1:T(8,128)(2,1)S(1)} %copy-done), kind=kOutput, calls=%fused_computation.87 | convolution fusion | flops 1274019840 | bytes 14063616 | tf_op jit(solution)/shard_map/dot_general | solution.py:131
  293.4 1.6 squeeze.18
  295.0 3.3 copy.66
  299.3 6.1 %fusion.42 = f32[4608,108]{1,0:T(8,128)S(1)} fusion(bf16[4608,1280]{1,0:T(8,128)(2,1)} %reshape.488, bf16[1280,108]{0,1:T(8,128)(2,1)S(1)} %copy-done.11), kind=kOutput, calls=%fused_computation.88 | convolution fusion | flops 1274019840 | bytes 14063616 | tf_op jit(solution)/shard_map/dot_general | solution.py:132
  305.4 1.6 squeeze.19
  307.0 3.3 copy.68
  313.9 2.5 scatter_fusion
  317.3 13.0 %reduce-scatter.3.cloned.1.call-done = f32[128,9,108]{0,2,1:T(8,128)} async-done(((f32[128,36,108]{0,2,1:T(8,128)}), f32[128,9,108]{0,2,1:T(8,128)}) %reduce-scatter.3.cloned.1.call-update) | async-done | bytes 497680 | tf_op jit(solution)/shard_map/reduce_scatter | solution.py:137
  330.3 40.0 %reduce-scatter.5.cloned.1.call-done = f32[128,9,108]{0,2,1:T(8,128)} async-done(((f32[128,36,108]{0,2,1:T(8,128)}), f32[128,9,108]{0,2,1:T(8,128)}) %reduce-scatter.5.cloned.1.call-update) | async-done | bytes 497680 | tf_op jit(solution)/shard_map/reduce_scatter | solution.py:138
  370.3 2.0 multiply_convert_fusion
  (90 shorter events, 17.5 us)
Async XLA Ops:
  7.2 280.1 %copy-start = (bf16[1280,108]{0,1:T(8,128)(2,1)S(1)}, bf16[1280,108]{0,1:T(8,128)(2,1)}, u32[]{:S(2)}) copy-start(bf16[1280,108]{0,1:T(8,128)(2,1)} %param.19) | copy-start | bytes 829444
  7.2 1.7 copy-start.9
  8.6 10.0 %copy-start.12 = (f32[1280]{0:T(1024)S(1)}, f32[1280]{0:T(1024)}, u32[]{:S(2)}) copy-start(f32[1280]{0:T(1024)} %param.17) | copy-start | bytes 15364
  21.3 2.0 copy-start.13
  26.0 2.7 copy-start.15
  26.0 3.7 copy-start.2
  26.0 6.2 %copy-start.5 = (bf16[256,1280]{1,0:T(8,128)(2,1)S(1)}, bf16[256,1280]{1,0:T(8,128)(2,1)}, u32[]{:S(2)}) copy-start(bf16[256,1280]{1,0:T(8,128)(2,1)} %param.15) | copy-start | bytes 1966084
  33.2 2.3 copy-start.4
  35.2 1.3 copy-start.3
  36.5 1.5 copy-start.7
  38.0 4.1 %copy-start.10 = (bf16[256,1280]{0,1:T(8,128)(2,1)S(1)}, bf16[256,1280]{0,1:T(8,128)(2,1)}, u32[]{:S(2)}) copy-start(bf16[256,1280]{0,1:T(8,128)(2,1)} %copy.62) | copy-start | bytes 1966084
  45.2 10.9 %copy-start.14 = (f32[1280]{0:T(1024)S(1)}, f32[1280]{0:T(1024)}, u32[]{:S(2)}) copy-start(f32[1280]{0:T(1024)} %param.18) | copy-start | bytes 15364
  61.3 59.9 %all-to-all-start = ((bf16[128,2,1280]{2,1,0:T(2,128)(2,1)}), bf16[128,2,1280]{2,1,0:T(2,128)(2,1)S(1)}, u32[]{:S(2)}, u32[]{:S(2)}) async-start(bf16[128,2,1280]{2,1,0:T(2,128)(2,1)} %broadcast_select_fusion), calls=%async_computation | async-start | bytes 1310720 | tf_op jit(solution)/shard_map/all_to_all | solution.py:47
  84.8 185.6 %all-gather.3.cloned.1.call-start = ((), (), s32[]{:S(2)}) async-start(), calls=%async_computation.5 | async-start | bytes 13209600 | tf_op jit(solution)/shard_map/all_gather | solution.py:128
  123.7 206.6 %reduce-scatter.3.cloned.1.call-start = ((), (), s32[]{:S(2)}) async-start(), calls=%async_computation.3 | async-start | bytes 2580480 | tf_op jit(solution)/shard_map/reduce_scatter | solution.py:137
  298.3 1.0 copy-start.11
  298.4 72.0 %reduce-scatter.5.cloned.1.call-start = ((), (), s32[]{:S(2)}) async-start(), calls=%async_computation.4 | async-start | bytes 2580480 | tf_op jit(solution)/shard_map/reduce_scatter | solution.py:138
  310.3 1.1 copy-start.8
  311.4 1.4 copy-start.16
  316.5 55.8 %copy-start.1 = (bf16[1280,108]{0,1:T(8,128)(2,1)S(1)}, bf16[1280,108]{0,1:T(8,128)(2,1)}, u32[]{:S(2)}) copy-start(bf16[1280,108]{0,1:T(8,128)(2,1)} %param.19) | copy-start | bytes 829444
  317.3 55.0 %copy-start.6 = (bf16[2,128,1280]{2,1,0:T(8,128)(2,1)}, bf16[2,128,1280]{2,1,0:T(8,128)(2,1)S(1)}, u32[]{:S(2)}) copy-start(bf16[2,128,1280]{2,1,0:T(8,128)(2,1)S(1)} %scatter_fusion.1) | copy-start | bytes 1966084
Sparse Core Ops, SparseCore 0:
  123.9 146.5 all-gather.2
  298.5 31.7 reduce-scatter.2
  333.4 36.8 reduce-scatter.4
where the time goes:
time: 380 us; the launch traced here: 379 us
  waiting for transfers between devices  235 us (62%)
  local copies, waits for them, and re-layouts  57.6 us (15%)
  starting transfers between devices  23.6 us (6%)
  matrix products  19.5 us (5%)
  blocking collectives  15.3 us (4%)
  between operations  14.1 us (4%)
  other arithmetic  13.3 us (4%)
    all_gather x1, waiting for transfers between devices, per_device(): piece = lax.all_gather(regrouped, 'req', axis=0, tiled=True)  147 us
    reduce_scatter x1, waiting for transfers between devices, per_device(): lax.psum_scatter(stacked[1], 'wt', scatter_dimension=1, tiled=True)  40 us
    all_to_all x1, waiting for transfers between devices, deal_rows(): lax.all_to_all(picked, 'req', split_axis=0, concat_axis=0, tiled=True)  35.7 us
    unnamed x42, local copies, waits for them, and re-layouts  29.6 us
    all_to_all x1, starting transfers between devices, deal_rows(): lax.all_to_all(picked, 'req', split_axis=0, concat_axis=0, tiled=True)  23.5 us
    reduce_scatter x1, waiting for transfers between devices, per_device(): lax.psum_scatter(stacked[0], 'wt', scatter_dimension=1, tiled=True)  13 us
    psum x1, blocking collectives, per_device(): lax.psum((jnp.sum(query_f * query_f, axis=1), jnp.sum(key_f * key_f, axis...  9.29 us
  transfers between devices with their start and end apart: 4, of which 4 were waited for; matrix products, arithmetic and copies ran while one was open for 5% of the time, Pallas kernels for 0%

commit v1 on v0

--- a/solution.py
+++ b/solution.py
@@ -9,6 +9,9 @@
 LIVE = 36
 EPS = 1e-06
 THETA = 500000.0
+hold_sample_in = lambda frame_in, row_dim: jnp.concatenate(
+    lax.all_to_all(jnp.stack(lax.axis_size("req") * [frame_in]), "req", 0, 0), axis=row_dim
+)
 
 
 def rope_tables(row_count, head_width):
@@ -125,7 +128,7 @@
     key_cache = jnp.zeros_like(key_pages).at[placement].set(key_pages)
     value_cache = jnp.zeros_like(value_pages).at[placement].set(value_pages)
     regrouped = deal_rows(layer_rows, owner_start, owner_len, device, owners, LIVE)
-    piece = lax.all_gather(regrouped, "req", axis=0, tiled=True)
+    piece = hold_sample_in(regrouped, row_dim=0)
     stacked = jnp.stack(
         [
             jnp.dot(piece, gate_w, preferred_element_type=jnp.float32),

time: 380 us -> 793 us (2.09)
  blocking collectives: 15.3 us -> 595 us
  waiting for transfers between devices: 235 us -> 90.8 us
  local copies, waits for them, and re-layouts: 57.6 us -> 36 us
    all_to_all x0 -> x1, blocking collectives: none -> 580 us  [lax.all_to_all(jnp.stack(lax.axis_size('req') * [frame_in]), 'req', 0, 0)]
    all_gather x1 -> x0, waiting for transfers between devices: 147 us -> none  [per_device(): piece = lax.all_gather(regrouped, 'req', axis=0, tiled=True)]
    unnamed x42 -> x41, local copies, waits for them, and re-layouts: 29.6 us -> 16.5 us
    squeeze x4 -> x0, local copies, waits for them, and re-layouts: 9.86 us -> none  [the longest x2 4.94 us: per_device(): stacked[1]]
  transfers between devices with their start and end apart: 4 -> 3, of which waited for: 4 -> 3; matrix products, arithmetic and copies ran while one was open for 5% -> 2% of each run, Pallas kernels for 0% -> 0%
where the time goes in v1:
time: 793 us; the launch traced here: 792 us
  blocking collectives  595 us (75%)
  waiting for transfers between devices  90.8 us (11%)
  local copies, waits for them, and re-layouts  36 us (5%)
  starting transfers between devices  23.8 us (3%)
  matrix products  21.5 us (3%)
  between operations  14.5 us (2%)
  other arithmetic  10.9 us (1%)
    all_to_all x1, blocking collectives, lax.all_to_all(jnp.stack(lax.axis_size('req') * [frame_in]), 'req', 0, 0)  580 us
    reduce_scatter x1, waiting for transfers between devices, per_device(): lax.psum_scatter(stacked[1], 'wt', scatter_dimension=1, tiled=True)  40 us
    all_to_all x1, waiting for transfers between devices, deal_rows(): lax.all_to_all(picked, 'req', split_axis=0, concat_axis=0, tiled=True)  35.7 us
    all_to_all x1, starting transfers between devices, deal_rows(): lax.all_to_all(picked, 'req', split_axis=0, concat_axis=0, tiled=True)  23.5 us
    unnamed x41, local copies, waits for them, and re-layouts  16.5 us
  transfers between devices with their start and end apart: 3, of which 3 were waited for; matrix products, arithmetic and copies ran while one was open for 2% of the time, Pallas kernels for 0%

profile of v1, /device:TPU:1, one launch (start us, length us, event | category | flops | bytes accessed | tf_op | source)
XLA Modules:
  0.0 792.4 jit_solution(4387744597601103627)
XLA Ops:
  7.2 1.4 copy.49
  9.3 9.3 %all-reduce = (f32[256]{0:T(256)S(1)}, f32[256]{0:T(256)S(1)}) all-reduce(f32[256]{0:T(256)S(1)} %fusion.9, f32[256]{0:T(256)S(1)} %fusion.7), channel_id=1, replica_groups=mesh['req'=128,'wt'=4] {'wt'}, use_global_device_ids=true, to_apply=%region_5.6 | all-reduce | flops 512 | bytes 4096 | tf_op jit(solution)/shard_map/psum | solution.py:88
  18.8 0.9 fusion.43
  19.8 1.5 copy.67
  21.3 1.5 copy.68
  23.6 1.5 copy.65
  25.1 1.5 copy.66
  26.6 1.0 scatter_custom_fusion
  27.6 1.2 gather_fusion.1
  30.2 2.2 copy.55
  34.6 2.7 fusion.44
  37.3 3.2 multiply_reduce_fusion
  40.5 1.7 copy.57
  42.3 6.0 psum.23
  48.7 1.2 gather_fusion
  51.4 1.4 add_convert_fusion
  52.8 1.3 gather_fusion.2
  54.3 0.7 add_compare_fusion.2
  55.2 1.5 broadcast_select_fusion
  56.7 23.5 %all-to-all-start = ((bf16[128,2,1280]{2,1,0:T(2,128)(2,1)}), bf16[128,2,1280]{2,1,0:T(2,128)(2,1)S(1)}, u32[]{:S(2)}, u32[]{:S(2)}) async-start(bf16[128,2,1280]{2,1,0:T(2,128)(2,1)} %broadcast_select_fusion), calls=%async_computation | async-start | bytes 1310720 | tf_op jit(solution)/shard_map/all_to_all | solution.py:50
  80.9 35.7 %all-to-all-done = bf16[128,2,1280]{2,1,0:T(2,128)(2,1)S(1)} async-done(((bf16[128,2,1280]{2,1,0:T(2,128)(2,1)}), bf16[128,2,1280]{2,1,0:T(2,128)(2,1)S(1)}, u32[]{:S(2)}, u32[]{:S(2)}) %all-to-all-start) | async-done | bytes 655392 | tf_op jit(solution)/shard_map/all_to_all | solution.py:50
  116.9 1.6 scatter_custom_fusion.1
  118.5 5.5 stack.2
  124.0 579.6 %all_to_all.10 = bf16[128,36,1280]{2,1,0:T(8,128)(2,1)S(1)} all-to-all(bf16[128,36,1280]{2,1,0:T(8,128)(2,1)} %stack.2), channel_id=1, replica_groups=mesh['req'=128,'wt'=4] {'req'}, dimensions={0} | all-to-all | bytes 23592960 | tf_op jit(solution)/shard_map/all_to_all | solution.py:13
  703.5 4.7 copy-done.2
  708.2 5.4 fusion.3
  714.6 10.2 %fusion.1 = f32[128,36,108]{0,2,1:T(8,128)} fusion(bf16[128,36,1280]{2,1,0:T(8,128)(2,1)} %copy-done.2, bf16[1280,108]{0,1:T(8,128)(2,1)S(1)} %copy-done.14), kind=kOutput, calls=%fused_computation.8 | convolution fusion | flops 1274019840 | bytes 14063616 | tf_op jit(solution)/shard_map/dot_general | solution.py:135
  726.5 0.7 scatter_fusion
  727.7 0.7 scatter_fusion.1
  728.5 15.0 %reduce-scatter.3.cloned.1.call-done = f32[128,9,108]{0,2,1:T(8,128)} async-done(((f32[128,36,108]{0,2,1:T(8,128)}), f32[128,9,108]{0,2,1:T(8,128)}) %reduce-scatter.3.cloned.1.call-update) | async-done | bytes 497680 | tf_op jit(solution)/shard_map/reduce_scatter | solution.py:140
  743.5 40.0 %reduce-scatter.5.cloned.1.call-done = f32[128,9,108]{0,2,1:T(8,128)} async-done(((f32[128,36,108]{0,2,1:T(8,128)}), f32[128,9,108]{0,2,1:T(8,128)}) %reduce-scatter.5.cloned.1.call-update) | async-done | bytes 497680 | tf_op jit(solution)/shard_map/reduce_scatter | solution.py:141
  783.5 2.0 multiply_convert_fusion
  (84 shorter events, 11.6 us)
Async XLA Ops:
  7.2 701.0 %copy-start = (bf16[1280,108]{0,1:T(8,128)(2,1)S(1)}, bf16[1280,108]{0,1:T(8,128)(2,1)}, u32[]{:S(2)}) copy-start(bf16[1280,108]{0,1:T(8,128)(2,1)} %param.19) | copy-start | bytes 829444
  7.2 1.7 copy-start.9
  8.6 10.0 %copy-start.11 = (f32[1280]{0:T(1024)S(1)}, f32[1280]{0:T(1024)}, u32[]{:S(2)}) copy-start(f32[1280]{0:T(1024)} %param.17) | copy-start | bytes 15364
  21.3 2.0 copy-start.12
  25.1 1.5 copy-start.15
  25.1 2.5 copy-start.1
  26.6 5.8 copy-start.3
  32.4 1.3 copy-start.5
  32.7 1.4 copy-start.4
  34.6 2.7 copy-start.10
  40.5 10.9 %copy-start.13 = (f32[1280]{0:T(1024)S(1)}, f32[1280]{0:T(1024)}, u32[]{:S(2)}) copy-start(f32[1280]{0:T(1024)} %param.18) | copy-start | bytes 15364
  56.7 59.9 %all-to-all-start = ((bf16[128,2,1280]{2,1,0:T(2,128)(2,1)}), bf16[128,2,1280]{2,1,0:T(2,128)(2,1)S(1)}, u32[]{:S(2)}, u32[]{:S(2)}) async-start(bf16[128,2,1280]{2,1,0:T(2,128)(2,1)} %broadcast_select_fusion), calls=%async_computation | async-start | bytes 1310720 | tf_op jit(solution)/shard_map/all_to_all | solution.py:50
  80.2 663.3 %reduce-scatter.3.cloned.1.call-start = ((), (), s32[]{:S(2)}) async-start(), calls=%async_computation.4 | async-start | bytes 2580480 | tf_op jit(solution)/shard_map/reduce_scatter | solution.py:140
  703.5 4.7 copy-start.2
  713.6 1.0 copy-start.14
  713.6 69.9 %reduce-scatter.5.cloned.1.call-start = ((), (), s32[]{:S(2)}) async-start(), calls=%async_computation.5 | async-start | bytes 2580480 | tf_op jit(solution)/shard_map/reduce_scatter | solution.py:141
  724.7 1.6 copy-start.16
  726.4 1.1 copy-start.6
  727.5 0.9 copy-start.8
  728.5 57.1 %copy-start.7 = (bf16[2,128,1280]{2,1,0:T(8,128)(2,1)}, bf16[2,128,1280]{2,1,0:T(8,128)(2,1)S(1)}, u32[]{:S(2)}) copy-start(bf16[2,128,1280]{2,1,0:T(8,128)(2,1)S(1)} %scatter_fusion.1) | copy-start | bytes 1966084
Sparse Core Ops, SparseCore 0:
  713.8 29.6 reduce-scatter.2
  746.6 36.8 reduce-scatter.4
